TPU v7x, 256 devices: a whole 4x4x8 slice. The times are simulated.
256 devices in a mesh: row: 32 (over x, z), col: 8 (over y, core).
Axes of the slice: x: 4, y: 4, z: 8, core: 2. Of those that a mesh axis runs over, the one named last changes fastest.
Arguments:
- points: float32 [16384, 256], P('row'), may hold values from -6 to 6
- nugget: float32 [16384], P('row'), may hold values from 0.5 to 2
- weights: float32 [256], replicated, may hold values from 0.0005 to 0.005
- band_start: int32 [32], replicated, may hold values from 0 to 30, as said below
Outputs:
- factored: float32 [32, 4, 8, 512, 512], P('row', None, 'col')
Inputs may be any that keep to these rules, and one draw needn't show every extreme that they name: band_start[i] <= i - 1 for every i >= 1, band_start[0] = 0; band_start[17] = 0; the last tile row has band_start = 30.
All inputs are finite; a program needn't handle non-finite values.
Results may differ from a plain program's by a relative error of at most 0.0003.
Values sent between devices are 32-bit elements; how exact they have to be, the bound alone decides.
No kernel may reach another device: no remote copies, remote signals or barrier semaphores. Data moves between devices by JAX's collectives and lax.ppermute only.
A program may use at most 128 MiB of HBM per device.

v0:
```python
import jax
import jax.numpy as jnp
from jax import lax
from jax.sharding import PartitionSpec as P

HI = lax.Precision.HIGHEST


def mm(a, b):
    return lax.dot_general(
        a, b, (((1,), (1,)), ((), ())), precision=HI, preferred_element_type=jnp.float32
    )


def kernel_tile(xrow, xcol, weights):
    weighted = xrow * weights
    sq_row = jnp.sum(weighted * xrow, axis=1)
    sq_col = jnp.sum(xcol * xcol * weights, axis=1)
    cross = mm(weighted, xcol)
    dist_sq = jnp.maximum(sq_row[:, None] + sq_col[None, :] - 2.0 * cross, 0.0)
    dist = jnp.sqrt(3.0 * dist_sq)
    return (1.0 + dist) * jnp.exp(-dist)


def chol_inv(a):
    low = jnp.linalg.cholesky(a)
    eye = jnp.eye(a.shape[0], dtype=a.dtype)
    inv = jax.scipy.linalg.solve_triangular(low, eye, lower=True)
    return (low, inv)


def body(points, nugget, weights, band_start):
    n_row = lax.axis_size("row")
    n_col = lax.axis_size("col")
    blocks = n_row // n_col
    tile = points.shape[0]
    piece = tile // n_row
    my_row = lax.axis_index("row")
    my_col = lax.axis_index("col")
    chunks = points.reshape(n_row, piece, points.shape[1])
    recv = lax.all_to_all(chunks, "row", 0, 0, tiled=True)
    mine = lax.dynamic_slice_in_dim(
        recv.reshape(blocks, n_col, piece, points.shape[1]), my_col, 1, axis=1
    )[:, 0]
    sel = jnp.concatenate([recv[:2], mine], axis=0)
    tiles_x = lax.all_gather(sel, "row", axis=1, tiled=True)
    nug = lax.all_gather(nugget, "row", tiled=True)
    x0, x1 = (tiles_x[0], tiles_x[1])
    xcols = tiles_x[2:]
    n0, n1 = (nug[:tile], nug[tile : 2 * tile])
    cols = my_col + n_col * jnp.arange(blocks, dtype=jnp.int32)
    rows = jnp.concatenate([my_row[None], cols])
    xr_all = jnp.concatenate([points[None], xcols], axis=0).reshape(-1, points.shape[1])
    nr = len(rows)
    eye = jnp.eye(tile, dtype=jnp.float32)
    x01 = jnp.concatenate([x0, x1], axis=0)
    k01 = kernel_tile(x01, x01, weights)
    a00 = k01[:tile, :tile] + eye * n0[None, :]
    a10 = k01[tile:, :tile]
    a11 = k01[tile:, tile:] + eye * n1[None, :]
    kr = kernel_tile(xr_all, x01, weights).reshape(nr, tile, 2, tile)
    bs = band_start[rows]
    keep0 = (bs <= 0)[:, None, None]
    keep1 = ((bs <= 1) & (rows >= 1))[:, None, None]
    ar0 = jnp.where(keep0, kr[:, :, 0], 0.0)
    ar0 = ar0 + jnp.where((rows == 0)[:, None, None], eye * n0[None, :], 0.0)
    ar1 = jnp.where(keep1, kr[:, :, 1], 0.0)
    ar1 = ar1 + jnp.where((rows == 1)[:, None, None], eye * n1[None, :], 0.0)
    l00, m0 = chol_inv(a00)
    stack0 = jnp.concatenate([a10, ar0.reshape(-1, tile)], axis=0)
    sol0 = mm(stack0, m0)
    l01 = sol0[:tile]
    lr0 = sol0[tile:].reshape(nr, tile, tile)
    lr0 = jnp.where((rows == 0)[:, None, None], l00[None], lr0)
    s11 = a11 - mm(l01, l01)
    upd1 = mm(lr0.reshape(-1, tile), l01).reshape(nr, tile, tile)
    ar1 = ar1 - jnp.where((rows >= 1)[:, None, None], upd1, 0.0)
    l11, m1 = chol_inv(s11)
    lr1 = mm(ar1.reshape(-1, tile), m1).reshape(nr, tile, tile)
    lr1 = jnp.where(
        (rows > 1)[:, None, None], lr1, jnp.where((rows == 1)[:, None, None], l11[None], 0.0)
    )
    kout = kernel_tile(points, xcols.reshape(-1, points.shape[1]), weights)
    kout = kout.reshape(tile, blocks, tile).transpose(1, 0, 2)
    bsr = band_start[my_row]
    keep = ((cols >= bsr) & (cols <= my_row))[:, None, None]
    aout = jnp.where(keep, kout, 0.0)
    aout = aout + jnp.where((cols == my_row)[:, None, None], eye * nugget[None, :], 0.0)
    left = jnp.concatenate([lr0[0], lr1[0]], axis=1)
    right = jnp.concatenate([lr0[1:], lr1[1:]], axis=2).reshape(-1, 2 * tile)
    prod = mm(left, right).reshape(tile, blocks, tile).transpose(1, 0, 2)
    live = ((cols > 1) & (cols <= my_row))[:, None, None]
    res = aout - jnp.where(live, prod, 0.0)
    res = jnp.where((cols == 0)[:, None, None], lr0[0][None], res)
    res = jnp.where((cols == 1)[:, None, None], lr1[0][None], res)
    return res.reshape(1, blocks, 1, tile, tile)


def solution(mesh):
    placed = (P("row", None), P("row"), P(), P())
    return jax.shard_map(
        body,
        mesh=mesh,
        in_specs=placed,
        out_specs=P("row", None, "col", None, None),
        check_vma=False,
    )
```

profile of v0, /device:TPU:8, one launch (start us, length us, event | category | flops | bytes accessed | tf_op | source)
XLA Modules:
  0.0 564.2 jit_solution(12527684723368307736)
XLA Ops:
  6.5 11.4 %all-to-all-start = ((f32[32,16,256]{2,1,0:T(8,128)}), f32[32,16,256]{2,1,0:T(8,128)S(1)}, u32[]{:S(2)}, u32[]{:S(2)}) async-start(f32[32,16,256]{2,1,0:T(8,128)} %bitcast.199), calls=%async_computation | async-start | bytes 1048576 | tf_op jit(solution)/shard_map/all_to_all | solution.py:41
  18.1 16.6 %all-to-all-done = f32[32,16,256]{2,1,0:T(8,128)S(1)} async-done(((f32[32,16,256]{2,1,0:T(8,128)}), f32[32,16,256]{2,1,0:T(8,128)S(1)}, u32[]{:S(2)}, u32[]{:S(2)}) %all-to-all-start) | async-done | bytes 524320 | tf_op jit(solution)/shard_map/all_to_all | solution.py:41
  37.1 48.4 %all-gather = f32[32,1,512]{2,1,0:T(1,128)S(1)} all-gather(f32[1,1,512]{2,1,0:T(1,128)} %bitcast.205), channel_id=1, replica_groups=mesh['row'=32,'col'=8] {'row'}, dimensions={0}, use_global_device_ids=true | all-gather | bytes 67584 | tf_op jit(solution)/shard_map/all_gather | solution.py:47
  90.2 22.2 %all-gather.3.cloned.1.call-done = f32[6,512,256]{2,1,0:T(8,128)} async-done(((f32[6,16,256]{2,1,0:T(8,128)}), f32[6,512,256]{2,1,0:T(8,128)}) %all-gather.3.cloned.1.call-update) | async-done | bytes 3145744 | tf_op jit(solution)/shard_map/all_gather | solution.py:46
  114.0 5.7 %exponential_multiply_fusion.2 = f32[1024,1024]{0,1:T(8,128)S(1)} fusion(f32[1024]{0:T(1024)S(1)} %get-tuple-element.24, f32[1024]{0:T(1024)S(1)} %get-tuple-element.23, f32[256]{0:T(256)S(1)} %copy-done.21, f32[512,256]{1,0:T(8,128)S(1)} %get-tuple-element.58, f32[512,256]{1,0:T(8,128)S(1)} %get-tuple-element.57), kind=kOutput, calls=%fused_computation.34 | convolution fusion | flops 3230400512 | bytes 5252096 | tf_op jit(solution)/shard_map/dot_general | solution.py:10
  123.9 11.9 %cholesky.286 = f32[128,128]{1,0:T(8,128)S(1)} custom-call(f32[128,128]{1,0:T(8,128)S(1)} %cholesky.426), custom_call_target="Cholesky" | custom-call | tf_op jit(solution)/shard_map/jit(cholesky)/cholesky | solution.py:26
  136.0 9.8 %custom-call.27 = f32[1,128,128]{1,2,0:T(8,128)S(1)} custom-call(f32[1,128,128]{2,1,0:T(8,128)S(1)} %get-tuple-element.84), custom_call_target="InvertDiagBlocksLowerTriangular" | custom-call | tf_op jit(solution)/shard_map/jit(cholesky)/cholesky | solution.py:26
  148.3 11.7 %cholesky.305 = f32[128,128]{1,0:T(8,128)S(1)} custom-call(f32[128,128]{1,0:T(8,128)S(1)} %cholesky.430), custom_call_target="Cholesky" | custom-call | tf_op jit(solution)/shard_map/jit(cholesky)/cholesky | solution.py:26
  160.1 9.8 %custom-call.28 = f32[1,128,128]{1,2,0:T(8,128)S(1)} custom-call(f32[1,128,128]{2,1,0:T(8,128)S(1)} %get-tuple-element.81), custom_call_target="InvertDiagBlocksLowerTriangular" | custom-call | tf_op jit(solution)/shard_map/jit(cholesky)/cholesky | solution.py:26
  171.5 11.9 %cholesky.326 = f32[128,128]{1,0:T(8,128)S(1)} custom-call(f32[128,128]{1,0:T(8,128)S(1)} %cholesky.435), custom_call_target="Cholesky" | custom-call | tf_op jit(solution)/shard_map/jit(cholesky)/cholesky | solution.py:26
  184.1 9.8 %custom-call.29 = f32[1,128,128]{1,2,0:T(8,128)S(1)} custom-call(f32[1,128,128]{2,1,0:T(8,128)S(1)} %get-tuple-element.78), custom_call_target="InvertDiagBlocksLowerTriangular" | custom-call | tf_op jit(solution)/shard_map/jit(cholesky)/cholesky | solution.py:26
  195.3 11.7 %cholesky.343 = f32[128,128]{1,0:T(8,128)S(1)} custom-call(f32[128,128]{1,0:T(8,128)S(1)} %convolution_subtract_fusion.12), custom_call_target="Cholesky" | custom-call | tf_op jit(solution)/shard_map/jit(cholesky)/cholesky | solution.py:26
  212.1 12.3 %while.4 = (s32[]{:T(128)}, f32[512,512]{1,0:T(8,128)}, s32[4,2]{0,1:T(2,128)S(1)}, f32[4,128,128]{2,1,0:T(8,128)S(1)}, s32[]{:T(128)}) while((s32[]{:T(128)}, f32[512,512]{1,0:T(8,128)}, s32[4,2]{0,1:T(2,128)S(1)}, f32[4,128,128]{2,1,0:T(8,128)S(1)}, s32[]{:T(128)}) %tuple.69), condition=%wide.while_cond, body=%wide.while_body.sunk | while | flops 2 | bytes 131181 | solution.py:28
  224.5 39.3 %custom-call.30 = f32[4,128,128]{1,2,0:T(8,128)S(1)} custom-call(f32[4,128,128]{2,1,0:T(8,128)S(1)} %get-tuple-element.21), custom_call_target="InvertDiagBlocksLowerTriangular" | custom-call | tf_op jit(solution)/shard_map/jit(_solve_triangular)/triangular_solve | solution.py:28
  279.6 17.7 %exponential_multiply_fusion = f32[2560,1024]{1,0:T(8,128)} fusion(f32[2560,256]{1,0:T(8,128)} %bitcast_multiply_fusion, f32[1024]{0:T(1024)S(1)} %get-tuple-element.24, f32[2560]{0:T(1024)S(1)} %add.168, f32[512,256]{1,0:T(8,128)} %copy-done.15, f32[512,256]{1,0:T(8,128)S(1)} %copy-done.14), kind=kOutput, calls=%fused_computation.5 | convolution fusion | flops 8074297344 | bytes 14170112 | tf_op jit(solution)/shard_map/dot_general | solution.py:10
  297.4 14.3 %reshape.264 = f32[5,512,2,512]{3,2,1,0:T(2,128)} reshape(f32[2560,1024]{1,0:T(8,128)} %exponential_multiply_fusion) | data formatting | bytes 20971520 | tf_op jit(solution)/shard_map/reshape | solution.py:61
  311.7 13.6 %fusion.133 = (f32[5,512,1,512]{3,2,1,0:T(1,128)}, f32[5,512,1,512]{3,2,1,0:T(1,128)S(1)}) fusion(f32[5,512,2,512]{3,2,1,0:T(2,128)} %reshape.264), kind=kLoop, calls=%fused_computation.240 | loop fusion | bytes 20971520 | tf_op jit(solution)/shard_map/slice | solution.py:67
  331.0 3.6 fusion.13
  334.7 11.8 %fusion.4 = f32[3072,512]{1,0:T(8,128)S(1)} fusion(f32[2560,512]{1,0:T(8,128)S(1)} %fusion.13, f32[512,512]{1,0:T(8,128)S(1)} %copy-done.9, f32[128,512]{1,0:T(8,128)S(1)} %copy-done.16, f32[128,512]{1,0:T(8,128)S(1)} %fusion.108, f32[128,512]{1,0:T(8,128)S(1)} %fusion.110, f32[128,512]{1,0:T(8,128)S(1)} %fusion.85), kind=kOutput, calls=%fused_computation.10 | convolution fusion | flops 9666035712 | bytes 13631488 | tf_op jit(solution)/shard_map/dot_general | solution.py:10
  356.0 11.7 %cholesky.358 = f32[128,128]{1,0:T(8,128)S(1)} custom-call(f32[128,128]{1,0:T(8,128)S(1)} %cholesky.439), custom_call_target="Cholesky" | custom-call | tf_op jit(solution)/shard_map/jit(cholesky)/cholesky | solution.py:26
  367.8 9.8 %custom-call.31 = f32[1,128,128]{1,2,0:T(8,128)S(1)} custom-call(f32[1,128,128]{2,1,0:T(8,128)S(1)} %get-tuple-element.72), custom_call_target="InvertDiagBlocksLowerTriangular" | custom-call | tf_op jit(solution)/shard_map/jit(cholesky)/cholesky | solution.py:26
  380.2 11.9 %cholesky.377 = f32[128,128]{1,0:T(8,128)S(1)} custom-call(f32[128,128]{1,0:T(8,128)S(1)} %cholesky.443), custom_call_target="Cholesky" | custom-call | tf_op jit(solution)/shard_map/jit(cholesky)/cholesky | solution.py:26
  393.4 9.8 %custom-call.32 = f32[1,128,128]{1,2,0:T(8,128)S(1)} custom-call(f32[1,128,128]{2,1,0:T(8,128)S(1)} %get-tuple-element.69), custom_call_target="InvertDiagBlocksLowerTriangular" | custom-call | tf_op jit(solution)/shard_map/jit(cholesky)/cholesky | solution.py:26
  404.8 11.7 %cholesky.398 = f32[128,128]{1,0:T(8,128)S(1)} custom-call(f32[128,128]{1,0:T(8,128)S(1)} %cholesky.448), custom_call_target="Cholesky" | custom-call | tf_op jit(solution)/shard_map/jit(cholesky)/cholesky | solution.py:26
  417.2 9.8 %custom-call.33 = f32[1,128,128]{1,2,0:T(8,128)S(1)} custom-call(f32[1,128,128]{2,1,0:T(8,128)S(1)} %get-tuple-element.66), custom_call_target="InvertDiagBlocksLowerTriangular" | custom-call | tf_op jit(solution)/shard_map/jit(cholesky)/cholesky | solution.py:26
  428.4 12.1 %cholesky.415 = f32[128,128]{1,0:T(8,128)S(1)} custom-call(f32[128,128]{1,0:T(8,128)S(1)} %convolution_subtract_fusion.11), custom_call_target="Cholesky" | custom-call | tf_op jit(solution)/shard_map/jit(cholesky)/cholesky | solution.py:26
  445.2 11.6 %while.5 = (s32[]{:T(128)}, f32[512,512]{1,0:T(8,128)}, s32[4,2]{0,1:T(2,128)S(1)}, f32[4,128,128]{2,1,0:T(8,128)S(1)}, s32[]{:T(128)}) while((s32[]{:T(128)}, f32[512,512]{1,0:T(8,128)}, s32[4,2]{0,1:T(2,128)S(1)}, f32[4,128,128]{2,1,0:T(8,128)S(1)}, s32[]{:T(128)}) %tuple.77), condition=%wide.while_cond.clone, body=%wide.while_body.clone.sunk | while | flops 2 | bytes 131181 | solution.py:28
  456.8 39.3 %custom-call.34 = f32[4,128,128]{1,2,0:T(8,128)S(1)} custom-call(f32[4,128,128]{2,1,0:T(8,128)S(1)} %get-tuple-element.22), custom_call_target="InvertDiagBlocksLowerTriangular" | custom-call | tf_op jit(solution)/shard_map/jit(_solve_triangular)/triangular_solve | solution.py:28
  507.5 10.8 %fusion.48 = f32[5,512,512]{2,1,0:T(8,128)S(1)} fusion(f32[5,512,512]{2,1,0:T(8,128)S(1)} %bitcast.195, f32[3072,512]{1,0:T(8,128)} %copy-done.1), kind=kOutput, calls=%fused_computation.90 | convolution fusion | flops 8053063680 | bytes 11534336 | tf_op jit(solution)/shard_map/dot_general | solution.py:10
  518.3 9.8 %select_select_fusion = f32[5,512,512]{2,1,0:T(8,128)S(1)} fusion(f32[5,512,1,512]{3,2,1,0:T(1,128)S(1)} %bitcast.198, f32[5,512,512]{2,1,0:T(8,128)S(1)} %fusion.48, f32[512,512]{1,0:T(8,128)S(1)} %copy-done.19, f32[512,512]{1,0:T(8,128)S(1)} %copy-done.18, pred[5]{0:T(512)(128)(4,1)S(1)} %get-tuple-element.89, pred[5]{0:T(512)(128)(4,1)S(1)} %get-tuple-element.88, ...), kind=kOutput, calls=%fused_computation.23 | convolution fusion | flops 8063025152 | bytes 18874388 | tf_op jit(solution)/shard_map/dot_general | solution.py:10
  535.4 5.8 %exponential_multiply_fusion.1 = f32[512,2048]{1,0:T(8,128)S(1)} fusion(f32[2048,256]{1,0:T(8,128)S(1)} %bitcast.196, f32[2048]{0:T(1024)S(1)} %bitcast.207, f32[512]{0:T(512)S(1)} %fusion.72, f32[512,256]{1,0:T(8,128)S(1)} %copy-done.8, f32[256]{0:T(256)S(1)} %copy-done.21), kind=kOutput, calls=%fused_computation.33 | convolution fusion | flops 3229745152 | bytes 6827008 | tf_op jit(solution)/shard_map/dot_general | solution.py:10
  541.3 15.7 %fusion.21 = f32[1,4,1,512,512]{4,3,2,1,0:T(8,128)} fusion(f32[64,4,8,512]{3,2,1,0:T(8,128)S(1)} %bitcast.208, f32[512,512]{1,0:T(8,128)S(1)} %copy-done.17, f32[512,512]{1,0:T(8,128)S(1)} %slice_bitcast_fusion, f32[512,512]{1,0:T(8,128)S(1)} %slice_bitcast_fusion.1, pred[4]{0:T(512)(128)(4,1)S(1)} %get-tuple-element.95, ...), kind=kOutput, calls=%fused_computation.32 | convolution fusion | flops 12894863360 | bytes 19922964 | tf_op jit(solution)/shard_map/dot_general | solution.py:10
  (181 shorter events, 104.4 us)
Async XLA Ops:
  6.5 80.5 %copy-start = (s32[32]{0:T(128)S(1)}, s32[32]{0:T(128)}, u32[]{:S(2)}) copy-start(s32[32]{0:T(128)} %param.10) | copy-start | bytes 388
  6.5 81.1 %copy-start.22 = (f32[512]{0:T(512)S(1)}, f32[512]{0:T(512)}, u32[]{:S(2)}) copy-start(f32[512]{0:T(512)} %param.8) | copy-start | bytes 6148
  6.5 83.3 %copy-start.6 = (f32[512,256]{1,0:T(8,128)S(1)}, f32[512,256]{1,0:T(8,128)}, u32[]{:S(2)}) copy-start(f32[512,256]{1,0:T(8,128)} %param.7) | copy-start | bytes 1572868
  6.5 83.4 %copy-start.21 = (f32[256]{0:T(256)S(1)}, f32[256]{0:T(256)}, u32[]{:S(2)}) copy-start(f32[256]{0:T(256)} %param.9) | copy-start | bytes 3076
  6.5 28.2 %all-to-all-start = ((f32[32,16,256]{2,1,0:T(8,128)}), f32[32,16,256]{2,1,0:T(8,128)S(1)}, u32[]{:S(2)}, u32[]{:S(2)}) async-start(f32[32,16,256]{2,1,0:T(8,128)} %bitcast.199), calls=%async_computation | async-start | bytes 1048576 | tf_op jit(solution)/shard_map/all_to_all | solution.py:41
  18.0 94.4 %all-gather.3.cloned.1.call-start = ((), (), s32[]{:S(2)}) async-start(), calls=%async_computation.1 | async-start | bytes 3244032 | tf_op jit(solution)/shard_map/all_gather | solution.py:46
  113.6 6.1 %copy-start.13 = (f32[512,256]{1,0:T(8,128)}, f32[512,256]{1,0:T(8,128)S(1)}, u32[]{:S(2)}) copy-start(f32[512,256]{1,0:T(8,128)S(1)} %get-tuple-element.57) | copy-start | bytes 1572868
  113.6 6.1 %copy-start.15 = (f32[512,256]{1,0:T(8,128)}, f32[512,256]{1,0:T(8,128)S(1)}, u32[]{:S(2)}) copy-start(f32[512,256]{1,0:T(8,128)S(1)} %get-tuple-element.58) | copy-start | bytes 1572868
  119.7 2.6 copy-start.12
  122.9 1.0 copy-start.11
  263.8 4.2 copy-start.20
  268.4 9.0 %copy-start.7 = (f32[512,256]{1,0:T(8,128)S(1)}, f32[512,256]{1,0:T(8,128)}, u32[]{:S(2)}) copy-start(f32[512,256]{1,0:T(8,128)} %param.7) | copy-start | bytes 1572868
  277.4 2.2 copy-start.3
  277.9 1.7 copy-start.14
  331.0 3.7 copy-start.9
  331.0 3.7 copy-start.16
  346.4 2.6 copy-start.1
  355.0 1.0 copy-start.10
  500.8 17.5 %slice-start.1 = ((s8[5242880]{0:T(1024)(128)(4,1)}), s8[4194304]{0:T(1024)(128)(4,1)S(1)}, s32[]{:S(2)}) async-start(s8[5242880]{0:T(1024)(128)(4,1)} %bitcast.197), calls=%async_computation.3 | async-start | bytes 8388608
  503.8 14.5 %slice-start.2 = ((s8[5242880]{0:T(1024)(128)(4,1)}), s8[1048576]{0:T(1024)(128)(4,1)S(1)}, s32[]{:S(2)}) async-start(s8[5242880]{0:T(1024)(128)(4,1)} %bitcast.197), calls=%async_computation.4 | async-start | bytes 2097152
  507.4 10.8 %copy-start.18 = (f32[512,512]{1,0:T(8,128)S(1)}, f32[512,512]{1,0:T(8,128)}, u32[]{:S(2)}) copy-start(f32[512,512]{1,0:T(8,128)} %copy.44) | copy-start | bytes 3145732
  507.4 10.8 %copy-start.19 = (f32[512,512]{1,0:T(8,128)S(1)}, f32[512,512]{1,0:T(8,128)}, u32[]{:S(2)}) copy-start(f32[512,512]{1,0:T(8,128)} %get-tuple-element.42) | copy-start | bytes 3145732
  528.1 2.3 copy-start.5
  531.8 2.7 copy-start.2
  531.9 3.2 copy-start.4
  531.9 3.6 copy-start.8
  535.4 5.8 %slice-start = ((f32[5,512,512]{2,1,0:T(8,128)}), f32[4,512,512]{2,1,0:T(8,128)S(1)}, s32[]{:S(2)}) async-start(f32[5,512,512]{2,1,0:T(8,128)} %copy-done.2), calls=%async_computation.2 | async-start | bytes 8388608 | tf_op jit(solution)/shard_map/slice | solution.py:90
  535.4 5.8 %slice-start.3 = ((f32[5,512,512]{2,1,0:T(8,128)}), f32[4,512,512]{2,1,0:T(8,128)S(1)}, s32[]{:S(2)}) async-start(f32[5,512,512]{2,1,0:T(8,128)} %copy-done.5), calls=%async_computation.5 | async-start | bytes 8388608 | tf_op jit(solution)/shard_map/slice | solution.py:90
  535.4 5.8 %copy-start.17 = (f32[512,512]{1,0:T(8,128)S(1)}, f32[512,512]{1,0:T(8,128)}, u32[]{:S(2)}) copy-start(f32[512,512]{1,0:T(8,128)} %copy.59) | copy-start | bytes 3145732
Sparse Core Ops, SparseCore 0:
  35.5 76.7 all-gather.2
where the time goes:
time: 575 us; the launch traced here: 564 us
  other arithmetic  258 us (45%)
  matrix products  108 us (19%)
  local copies, waits for them, and re-layouts  78.9 us (14%)
  blocking collectives  48.4 us (8%)
  waiting for transfers between devices  38.8 us (7%)
  between operations  19.7 us (3%)
  starting transfers between devices  11.5 us (2%)
    another operation x29, other arithmetic, chol_inv(): low = jnp.linalg.cholesky(a)  158 us
    another operation x5, other arithmetic, chol_inv(): inv = jax.scipy.linalg.solve_triangular(low, eye, lower=True)  81.5 us
    dot_general x8, matrix products, mm(): lax.dot_general(a, b, (((1,), (1,)), ((), ())), precision=HI, preferred_e...  80.4 us
    all_gather x1, blocking collectives, body(): nug = lax.all_gather(nugget, 'row', tiled=True)  48.4 us
    another operation x27, local copies, waits for them, and re-layouts, chol_inv(): inv = jax.scipy.linalg.solve_triangular(low, eye, lower=True)  23.4 us
    all_gather x1, waiting for transfers between devices, body(): tiles_x = lax.all_gather(sel, 'row', axis=1, tiled=True)  22.2 us
    all_to_all x1, waiting for transfers between devices, body(): recv = lax.all_to_all(chunks, 'row', 0, 0, tiled=True)  16.6 us
    another operation x14, matrix products, chol_inv(): inv = jax.scipy.linalg.solve_triangular(low, eye, lower=True)  16.6 us
  transfers between devices with their start and end apart: 2, of which 2 were waited for; matrix products, arithmetic and copies ran while one was open for 1% of the time, Pallas kernels for 0%

commit v1 on v0

--- a/solution.py
+++ b/solution.py
@@ -44,7 +44,8 @@
     )[:, 0]
     sel = jnp.concatenate([recv[:2], mine], axis=0)
     tiles_x = lax.all_gather(sel, "row", axis=1, tiled=True)
-    nug = lax.all_gather(nugget, "row", tiled=True)
+    copies = jnp.concatenate([nugget] * lax.axis_size("row"), axis=0)
+    nug = lax.all_to_all(copies, "row", 0, 0, tiled=True)
     x0, x1 = (tiles_x[0], tiles_x[1])
     xcols = tiles_x[2:]
     n0, n1 = (nug[:tile], nug[tile : 2 * tile])

time: 575 us -> 628 us (1.092)
  blocking collectives: 48.4 us -> 0 us
  waiting for transfers between devices: 38.8 us -> 79 us
  local copies, waits for them, and re-layouts: 78.9 us -> 105 us
  other arithmetic: 258 us -> 276 us
  matrix products: 108 us -> 119 us
    all_gather x1 -> x0, blocking collectives: 48.4 us -> none  [body(): nug = lax.all_gather(nugget, 'row', tiled=True)]
    all_gather x1, waiting for transfers between devices: 22.2 us -> 58.5 us  [body(): tiles_x = lax.all_gather(sel, 'row', axis=1, tiled=True)]
    another operation x29, other arithmetic: 158 us -> 169 us  [chol_inv(): low = jnp.linalg.cholesky(a)]
    unnamed x52 -> x57, local copies, waits for them, and re-layouts: 14.4 us -> 25 us
    dot_general x8, matrix products: 80.4 us -> 87.9 us  [mm(): lax.dot_general(a, b, (((1,), (1,)), ((), ())), precision=HI, preferred_e...]
  transfers between devices with their start and end apart: 2 -> 3, of which waited for: 2 -> 3; matrix products, arithmetic and copies ran while one was open for 1% -> 1% of each run, Pallas kernels for 0% -> 0%
where the time goes in v1:
time: 628 us; the launch traced here: 616 us
  other arithmetic  276 us (44%)
  matrix products  119 us (19%)
  local copies, waits for them, and re-layouts  105 us (17%)
  waiting for transfers between devices  79 us (13%)
  between operations  19.7 us (3%)
  starting transfers between devices  17.3 us (3%)
    another operation x29, other arithmetic, chol_inv(): low = jnp.linalg.cholesky(a)  169 us
    dot_general x8, matrix products, mm(): lax.dot_general(a, b, (((1,), (1,)), ((), ())), precision=HI, preferred_e...  87.9 us
    another operation x5, other arithmetic, chol_inv(): inv = jax.scipy.linalg.solve_triangular(low, eye, lower=True)  82.1 us
    all_gather x1, waiting for transfers between devices, body(): tiles_x = lax.all_gather(sel, 'row', axis=1, tiled=True)  58.5 us
    unnamed x57, local copies, waits for them, and re-layouts  25 us
    another operation x27, local copies, waits for them, and re-layouts, chol_inv(): inv = jax.scipy.linalg.solve_triangular(low, eye, lower=True)  23 us
    another operation x14, matrix products, chol_inv(): inv = jax.scipy.linalg.solve_triangular(low, eye, lower=True)  20.6 us
    all_to_all x1, waiting for transfers between devices, body(): recv = lax.all_to_all(chunks, 'row', 0, 0, tiled=True)  16.7 us
  transfers between devices with their start and end apart: 3, of which 3 were waited for; matrix products, arithmetic and copies ran while one was open for 1% of the time, Pallas kernels for 0%

profile of v1, /device:TPU:8, one launch (start us, length us, event | category | flops | bytes accessed | tf_op | source)
XLA Modules:
  0.0 616.0 jit_solution(777780185831607041)
XLA Ops:
  6.5 11.4 %all-to-all-start = ((f32[32,16,256]{2,1,0:T(8,128)}), f32[32,16,256]{2,1,0:T(8,128)S(1)}, u32[]{:S(2)}, u32[]{:S(2)}) async-start(f32[32,16,256]{2,1,0:T(8,128)} %bitcast.194), calls=%async_computation | async-start | bytes 1048576 | tf_op jit(solution)/shard_map/all_to_all | solution.py:41
  18.0 16.7 %all-to-all-done = f32[32,16,256]{2,1,0:T(8,128)S(1)} async-done(((f32[32,16,256]{2,1,0:T(8,128)}), f32[32,16,256]{2,1,0:T(8,128)S(1)}, u32[]{:S(2)}, u32[]{:S(2)}) %all-to-all-start) | async-done | bytes 524320 | tf_op jit(solution)/shard_map/all_to_all | solution.py:41
  36.7 5.8 all-to-all-start.1
  53.8 58.5 %all-gather.2.cloned.1.call-done = f32[6,512,256]{2,1,0:T(8,128)} async-done(((f32[6,16,256]{2,1,0:T(8,128)}), f32[6,512,256]{2,1,0:T(8,128)}) %all-gather.2.cloned.1.call-update) | async-done | bytes 3145744 | tf_op jit(solution)/shard_map/all_gather | solution.py:46
  123.9 11.7 %cholesky.286 = f32[128,128]{1,0:T(8,128)S(1)} custom-call(f32[128,128]{1,0:T(8,128)S(1)} %cholesky.426), custom_call_target="Cholesky" | custom-call | tf_op jit(solution)/shard_map/jit(cholesky)/cholesky | solution.py:26
  135.8 10.0 %custom-call.27 = f32[1,128,128]{1,2,0:T(8,128)S(1)} custom-call(f32[1,128,128]{2,1,0:T(8,128)S(1)} %get-tuple-element.84), custom_call_target="InvertDiagBlocksLowerTriangular" | custom-call | tf_op jit(solution)/shard_map/jit(cholesky)/cholesky | solution.py:26
  148.3 11.7 %cholesky.305 = f32[128,128]{1,0:T(8,128)S(1)} custom-call(f32[128,128]{1,0:T(8,128)S(1)} %cholesky.430), custom_call_target="Cholesky" | custom-call | tf_op jit(solution)/shard_map/jit(cholesky)/cholesky | solution.py:26
  160.0 9.8 %custom-call.28 = f32[1,128,128]{1,2,0:T(8,128)S(1)} custom-call(f32[1,128,128]{2,1,0:T(8,128)S(1)} %get-tuple-element.81), custom_call_target="InvertDiagBlocksLowerTriangular" | custom-call | tf_op jit(solution)/shard_map/jit(cholesky)/cholesky | solution.py:26
  171.4 22.5 %cholesky.326 = f32[128,128]{1,0:T(8,128)S(1)} custom-call(f32[128,128]{1,0:T(8,128)S(1)} %cholesky.435), custom_call_target="Cholesky" | custom-call | tf_op jit(solution)/shard_map/jit(cholesky)/cholesky | solution.py:26
  194.7 9.8 %custom-call.29 = f32[1,128,128]{1,2,0:T(8,128)S(1)} custom-call(f32[1,128,128]{2,1,0:T(8,128)S(1)} %get-tuple-element.78), custom_call_target="InvertDiagBlocksLowerTriangular" | custom-call | tf_op jit(solution)/shard_map/jit(cholesky)/cholesky | solution.py:26
  206.0 11.7 %cholesky.343 = f32[128,128]{1,0:T(8,128)S(1)} custom-call(f32[128,128]{1,0:T(8,128)S(1)} %convolution_subtract_fusion.12), custom_call_target="Cholesky" | custom-call | tf_op jit(solution)/shard_map/jit(cholesky)/cholesky | solution.py:26
  222.9 12.0 %while.4 = (s32[]{:T(128)}, f32[512,512]{1,0:T(8,128)}, s32[4,2]{0,1:T(2,128)S(1)}, f32[4,128,128]{2,1,0:T(8,128)S(1)}, s32[]{:T(128)}) while((s32[]{:T(128)}, f32[512,512]{1,0:T(8,128)}, s32[4,2]{0,1:T(2,128)S(1)}, f32[4,128,128]{2,1,0:T(8,128)S(1)}, s32[]{:T(128)}) %tuple.69), condition=%wide.while_cond, body=%wide.while_body.sunk | while | flops 2 | bytes 131181 | solution.py:28
  234.8 39.3 %custom-call.30 = f32[4,128,128]{1,2,0:T(8,128)S(1)} custom-call(f32[4,128,128]{2,1,0:T(8,128)S(1)} %get-tuple-element.21), custom_call_target="InvertDiagBlocksLowerTriangular" | custom-call | tf_op jit(solution)/shard_map/jit(_solve_triangular)/triangular_solve | solution.py:28
  290.0 18.0 %exponential_multiply_fusion = f32[2560,1024]{1,0:T(8,128)} fusion(f32[2560,256]{1,0:T(8,128)} %bitcast_multiply_fusion, f32[1024]{0:T(1024)S(1)} %get-tuple-element.24, f32[2560]{0:T(1024)S(1)} %add.168, f32[512,256]{1,0:T(8,128)} %copy-done.19, f32[512,256]{1,0:T(8,128)S(1)} %copy-done.18), kind=kOutput, calls=%fused_computation.5 | convolution fusion | flops 8074297344 | bytes 14170112 | tf_op jit(solution)/shard_map/dot_general | solution.py:10
  308.0 14.3 %reshape.304 = f32[5,512,2,512]{3,2,1,0:T(2,128)} reshape(f32[2560,1024]{1,0:T(8,128)} %exponential_multiply_fusion) | data formatting | bytes 20971520 | tf_op jit(solution)/shard_map/reshape | solution.py:62
  322.3 13.5 %fusion.132 = (f32[5,512,1,512]{3,2,1,0:T(1,128)}, f32[5,512,1,512]{3,2,1,0:T(1,128)S(1)}) fusion(f32[5,512,2,512]{3,2,1,0:T(2,128)} %reshape.304), kind=kLoop, calls=%fused_computation.239 | loop fusion | bytes 20971520 | tf_op jit(solution)/shard_map/slice | solution.py:68
  345.2 11.6 %fusion.4 = f32[3072,512]{1,0:T(8,128)S(1)} fusion(f32[2560,512]{1,0:T(8,128)S(1)} %fusion.8, f32[512,512]{1,0:T(8,128)S(1)} %copy-done.8, f32[128,512]{1,0:T(8,128)S(1)} %copy-done.20, f32[128,512]{1,0:T(8,128)S(1)} %fusion.107, f32[128,512]{1,0:T(8,128)S(1)} %fusion.109, f32[128,512]{1,0:T(8,128)S(1)} %fusion.84), kind=kOutput, calls=%fused_computation.10 | convolution fusion | flops 9666035712 | bytes 13631488 | tf_op jit(solution)/shard_map/dot_general | solution.py:10
  366.3 11.7 %cholesky.358 = f32[128,128]{1,0:T(8,128)S(1)} custom-call(f32[128,128]{1,0:T(8,128)S(1)} %cholesky.439), custom_call_target="Cholesky" | custom-call | tf_op jit(solution)/shard_map/jit(cholesky)/cholesky | solution.py:26
  378.2 9.8 %custom-call.31 = f32[1,128,128]{1,2,0:T(8,128)S(1)} custom-call(f32[1,128,128]{2,1,0:T(8,128)S(1)} %get-tuple-element.72), custom_call_target="InvertDiagBlocksLowerTriangular" | custom-call | tf_op jit(solution)/shard_map/jit(cholesky)/cholesky | solution.py:26
  390.6 12.1 %cholesky.377 = f32[128,128]{1,0:T(8,128)S(1)} custom-call(f32[128,128]{1,0:T(8,128)S(1)} %cholesky.443), custom_call_target="Cholesky" | custom-call | tf_op jit(solution)/shard_map/jit(cholesky)/cholesky | solution.py:26
  404.0 9.8 %custom-call.32 = f32[1,128,128]{1,2,0:T(8,128)S(1)} custom-call(f32[1,128,128]{2,1,0:T(8,128)S(1)} %get-tuple-element.69), custom_call_target="InvertDiagBlocksLowerTriangular" | custom-call | tf_op jit(solution)/shard_map/jit(cholesky)/cholesky | solution.py:26
  415.3 11.7 %cholesky.398 = f32[128,128]{1,0:T(8,128)S(1)} custom-call(f32[128,128]{1,0:T(8,128)S(1)} %cholesky.448), custom_call_target="Cholesky" | custom-call | tf_op jit(solution)/shard_map/jit(cholesky)/cholesky | solution.py:26
  427.8 9.8 %custom-call.33 = f32[1,128,128]{1,2,0:T(8,128)S(1)} custom-call(f32[1,128,128]{2,1,0:T(8,128)S(1)} %get-tuple-element.66), custom_call_target="InvertDiagBlocksLowerTriangular" | custom-call | tf_op jit(solution)/shard_map/jit(cholesky)/cholesky | solution.py:26
  439.1 11.9 %cholesky.415 = f32[128,128]{1,0:T(8,128)S(1)} custom-call(f32[128,128]{1,0:T(8,128)S(1)} %convolution_subtract_fusion.11), custom_call_target="Cholesky" | custom-call | tf_op jit(solution)/shard_map/jit(cholesky)/cholesky | solution.py:26
  455.7 11.2 %while.5 = (s32[]{:T(128)}, f32[512,512]{1,0:T(8,128)}, s32[4,2]{0,1:T(2,128)S(1)}, f32[4,128,128]{2,1,0:T(8,128)S(1)}, s32[]{:T(128)}) while((s32[]{:T(128)}, f32[512,512]{1,0:T(8,128)}, s32[4,2]{0,1:T(2,128)S(1)}, f32[4,128,128]{2,1,0:T(8,128)S(1)}, s32[]{:T(128)}) %tuple.77), condition=%wide.while_cond.clone, body=%wide.while_body.clone.sunk | while | flops 2 | bytes 131181 | solution.py:28
  466.8 39.9 %custom-call.34 = f32[4,128,128]{1,2,0:T(8,128)} custom-call(f32[4,128,128]{2,1,0:T(8,128)S(1)} %get-tuple-element.22), custom_call_target="InvertDiagBlocksLowerTriangular" | custom-call | tf_op jit(solution)/shard_map/jit(_solve_triangular)/triangular_solve | solution.py:28
  525.5 12.3 %fusion.47 = f32[5,512,512]{1,2,0:T(8,128)} fusion(f32[5,512,512]{2,1,0:T(8,128)S(1)} %bitcast.192, f32[3072,512]{1,0:T(8,128)} %copy-done), kind=kOutput, calls=%fused_computation.89 | convolution fusion | flops 8053063680 | bytes 11534336 | tf_op jit(solution)/shard_map/dot_general | solution.py:10
  537.8 11.8 %copy.50 = f32[5,512,1,512]{1,3,0,2:T(8,128)} copy(f32[5,512,1,512]{3,2,1,0:T(1,128)} %get-tuple-element.51) | data formatting | bytes 10485760
  549.7 13.7 %select_select_fusion = f32[5,512,512]{1,2,0:T(8,128)S(1)} fusion(f32[5,512,1,512]{1,3,0,2:T(8,128)} %copy.50, f32[5,512,512]{1,2,0:T(8,128)} %fusion.47, f32[512,512]{0,1:T(8,128)} %copy.34, f32[512,512]{0,1:T(8,128)S(1)} %copy-done.21, pred[5]{0:T(512)(128)(4,1)S(1)} %get-tuple-element.89, pred[5]{0:T(512)(128)(4,1)S(1)} %get-tuple-element.88, ...), kind=kOutput, calls=%fused_computation.22 | convolution fusion | flops 8063025152 | bytes 18874388 | tf_op jit(solution)/shard_map/dot_general | solution.py:10
  567.1 6.1 copy.36
  585.2 5.8 exponential_multiply_fusion.1
  591.0 17.6 %fusion.20 = f32[1,4,1,512,512]{4,3,2,1,0:T(8,128)} fusion(f32[64,4,8,512]{3,2,1,0:T(8,128)S(1)} %bitcast.202, f32[512,512]{1,0:T(8,128)} %copy.39, f32[512,512]{1,0:T(8,128)} %copy.37, f32[512,512]{1,0:T(8,128)} %copy.35, pred[4]{0:T(512)(128)(4,1)S(1)} %get-tuple-element.95, pred[4]{0:T(512)(128)(4,1)S(1)} %get-tuple-element.97, ...), kind=kOutput, calls=%fused_computation.31 | convolution fusion | flops 12894863360 | bytes 22020116 | tf_op jit(solution)/shard_map/dot_general | solution.py:10
  (191 shorter events, 135.7 us)
Async XLA Ops:
  6.5 42.0 %copy-start.5 = (f32[512,256]{1,0:T(8,128)S(1)}, f32[512,256]{1,0:T(8,128)}, u32[]{:S(2)}) copy-start(f32[512,256]{1,0:T(8,128)} %param.7) | copy-start | bytes 1572868
  6.5 42.0 %copy-start.26 = (f32[256]{0:T(256)S(1)}, f32[256]{0:T(256)}, u32[]{:S(2)}) copy-start(f32[256]{0:T(256)} %param.9) | copy-start | bytes 3076
  6.5 28.2 %all-to-all-start = ((f32[32,16,256]{2,1,0:T(8,128)}), f32[32,16,256]{2,1,0:T(8,128)S(1)}, u32[]{:S(2)}, u32[]{:S(2)}) async-start(f32[32,16,256]{2,1,0:T(8,128)} %bitcast.194), calls=%async_computation | async-start | bytes 1048576 | tf_op jit(solution)/shard_map/all_to_all | solution.py:41
  18.0 94.3 %all-gather.2.cloned.1.call-start = ((), (), s32[]{:S(2)}) async-start(), calls=%async_computation.2 | async-start | bytes 3244032 | tf_op jit(solution)/shard_map/all_gather | solution.py:46
  36.7 15.9 %all-to-all-start.1 = ((f32[32,512,1]{1,2,0:T(1,128)}), f32[32,512,1]{1,2,0:T(1,128)S(1)}, u32[]{:S(2)}, u32[]{:S(2)}) async-start(f32[32,512,1]{1,2,0:T(1,128)} %concatenate.87), calls=%async_computation.1 | async-start | bytes 131072 | tf_op jit(solution)/shard_map/all_to_all | solution.py:48
  113.6 6.1 copy-start.17
  113.6 6.1 copy-start.19
  119.7 2.6 copy-start.14
  122.9 1.0 copy-start.13
  274.2 4.2 copy-start.24
  278.8 9.0 %copy-start.6 = (f32[512,256]{1,0:T(8,128)S(1)}, f32[512,256]{1,0:T(8,128)}, u32[]{:S(2)}) copy-start(f32[512,256]{1,0:T(8,128)} %param.7) | copy-start | bytes 1572868
  287.8 2.2 copy-start.2
  288.3 1.7 copy-start.18
  341.6 3.7 copy-start.8
  341.6 3.7 copy-start.20
  356.8 2.7 copy-start
  365.4 1.0 copy-start.12
  455.6 62.9 %copy-start.9 = (f32[512,512]{1,0:T(8,128)S(1)}, f32[512,512]{1,0:T(8,128)}, u32[]{:S(2)}) copy-start(f32[512,512]{1,0:T(8,128)} %get-tuple-element.42) | copy-start | bytes 3145732
  510.8 5.8 copy-start.15
  514.1 4.5 copy-start.22
  537.8 11.8 %copy-start.16 = (f32[128,512]{1,0:T(8,128)S(1)}, f32[128,512]{1,0:T(8,128)}, u32[]{:S(2)}) copy-start(f32[128,512]{1,0:T(8,128)} %copy-done.15) | copy-start | bytes 786436
  537.8 11.8 %copy-start.21 = (f32[512,512]{0,1:T(8,128)S(1)}, f32[512,512]{0,1:T(8,128)}, u32[]{:S(2)}) copy-start(f32[512,512]{0,1:T(8,128)} %fusion.55) | copy-start | bytes 3145732
  537.8 11.8 %copy-start.23 = (f32[128,512]{1,0:T(8,128)S(1)}, f32[128,512]{1,0:T(8,128)}, u32[]{:S(2)}) copy-start(f32[128,512]{1,0:T(8,128)} %copy-done.22) | copy-start | bytes 786436
  537.8 11.8 %copy-start.25 = (f32[128,512]{1,0:T(8,128)S(1)}, f32[128,512]{1,0:T(8,128)}, u32[]{:S(2)}) copy-start(f32[128,512]{1,0:T(8,128)} %fusion.100) | copy-start | bytes 786436
  563.4 2.3 copy-start.4
  576.5 2.3 copy-start.1
  578.9 6.2 %copy-start.3 = (f32[4,512,256]{2,1,0:T(8,128)S(1)}, f32[4,512,256]{2,1,0:T(8,128)}, u32[]{:S(2)}) copy-start(f32[4,512,256]{2,1,0:T(8,128)} %copy-done.2) | copy-start | bytes 6291460
  578.9 6.2 %copy-start.7 = (f32[512,256]{1,0:T(8,128)S(1)}, f32[512,256]{1,0:T(8,128)}, u32[]{:S(2)}) copy-start(f32[512,256]{1,0:T(8,128)} %param.7) | copy-start | bytes 1572868
  585.1 5.9 slice-start
  585.1 5.9 slice-start.1
  585.1 5.9 copy-start.10
  585.1 5.9 copy-start.11
Sparse Core Ops, SparseCore 0:
  35.5 76.7 all-gather.1
